TPU v7x, 32 devices: a whole 2x2x4 slice. The times are simulated.
32 devices in a mesh: groups: 2 (over x), tensor: 16 (over z, y, core).
Axes of the slice: x: 2, y: 2, z: 4, core: 2. Of those that a mesh axis runs over, the one named last changes fastest.
Arguments:
- tokens: bfloat16 [256, 8192], P(('groups', 'tensor')), parts along dimension 0, may hold values from -6 to 6
- gate_weight: bfloat16 [8192, 28672], P(None, 'tensor'), may hold values from -0.0625 to 0.0625
- up_weight: bfloat16 [8192, 28672], P(None, 'tensor'), may hold values from -0.0625 to 0.0625
- adapter_down_weight: bfloat16 [16, 8192, 64], P('tensor'), may hold values from -0.0625 to 0.0625
- adapter_up_weight: bfloat16 [16, 64, 28672], P(None, None, 'tensor'), may hold values from -0.75 to 0.75
- token_adapter_index: int32 [256, 1], P(('groups', 'tensor')), parts along dimension 0, may hold values from 0 to 15; in each aligned block of 128 rows (0 to 127, 128 to 255, ...) at most 16 rows name the same one
- adapter_slot_index: int32 [16], replicated, may hold values from 0 to 15, each once
Outputs:
- hidden: bfloat16 [256, 28672], P('groups', 'tensor'), parts along dimension 0
There are 2 independent parts, one for each index of `groups`. A program takes and returns all parts, laid end to end along the dimension named above; an argument that names none is the same for every part. Nothing has to cross between parts.
Inputs may be any that keep to these rules, and one draw needn't show every extreme that they name: `token_adapter_index`: in every draw at most 16 of all 128 tokens use one adapter, and some adapter is used by exactly 16 tokens; every adapter is used by some token. `adapter_slot_index`: A permutation; slot s is stored on the device of index s along tensor.
All inputs are finite; a program needn't handle non-finite values.
Results may differ from a plain program's by a relative error of at most 0.0039.
Values may be sent and summed in bfloat16 or wider, within the bound.
No kernel may reach another device: no remote copies, remote signals or barrier semaphores. Data moves between devices by JAX's collectives and lax.ppermute only.
A program may use at most 192 MiB of HBM per device.

v0:
```python
import jax
import jax.numpy as jnp
from jax import lax
from jax.sharding import PartitionSpec as P

CHUNKS = 2
LANES = 128


def body(
    tokens,
    gate_weight,
    up_weight,
    adapter_down_weight,
    adapter_up_weight,
    token_adapter_index,
    adapter_slot_index,
):
    me = lax.axis_index("tensor")
    rows, width = tokens.shape
    step = width // CHUNKS
    local_slot = jnp.take(adapter_slot_index, token_adapter_index[:, 0], axis=0)
    slot_cols = jnp.broadcast_to(local_slot.astype(jnp.bfloat16)[:, None], (rows, LANES))
    gate = up = low = None
    slots = None
    for c in range(CHUNKS):
        piece = tokens[:, c * step : (c + 1) * step]
        if c == CHUNKS - 1:
            piece = jnp.concatenate([piece, slot_cols], axis=1)
        gathered = lax.all_gather(piece, "tensor", axis=0, tiled=True)
        if c == CHUNKS - 1:
            slots = gathered[:, step].astype(jnp.int32)
            gathered = gathered[:, :step]
        g = jnp.dot(
            gathered, gate_weight[c * step : (c + 1) * step], preferred_element_type=jnp.float32
        )
        u = jnp.dot(
            gathered, up_weight[c * step : (c + 1) * step], preferred_element_type=jnp.float32
        )
        d = jnp.dot(
            gathered,
            adapter_down_weight[0, c * step : (c + 1) * step],
            preferred_element_type=jnp.float32,
        )
        gate = g if gate is None else gate + g
        up = u if up is None else up + u
        low = d if low is None else low + d
    mine = slots == me
    low = jnp.where(mine[:, None], low, 0.0).astype(jnp.bfloat16)
    spread = lax.all_gather(low, "tensor", axis=0, tiled=False)
    delta = jnp.einsum("str,srh->th", spread, adapter_up_weight, preferred_element_type=jnp.float32)
    return (jax.nn.silu(gate) * (up + delta)).astype(jnp.bfloat16)


def solution(mesh):
    in_specs = (
        P(("groups", "tensor"), None),
        P(None, "tensor"),
        P(None, "tensor"),
        P("tensor", None, None),
        P(None, None, "tensor"),
        P(("groups", "tensor"), None),
        P(),
    )
    out_specs = P("groups", "tensor")
    return jax.shard_map(body, mesh=mesh, in_specs=in_specs, out_specs=out_specs, check_vma=False)
```

profile of v0, /device:TPU:0, one launch (start us, length us, event | category | flops | bytes accessed | tf_op | source)
XLA Modules:
  0.0 148.9 jit_solution(2792847004383480132)
XLA Ops:
  6.5 0.0 copy-start
  6.5 0.0 all-gather.4.cloned.1.call-start
  6.5 1.5 %fusion.40 = (bf16[8,4096]{1,0:T(8,128)(2,1)}, bf16[8,4096]{1,0:T(8,128)(2,1)S(1)}) fusion(bf16[8,8192]{1,0:T(8,128)(2,1)} %param.7), kind=kLoop, calls=%fused_computation.36 | loop fusion | bytes 262144 | tf_op jit(solution)/shard_map/slice | solution.py:27
  8.0 0.0 all-gather.4.cloned.1.call-update
  8.1 0.0 all-gather.6.cloned.1.call-start
  8.1 0.7 fusion.39
  8.8 0.0 copy-done
  8.8 0.6 gather_fusion
  9.4 0.7 convert_bitcast_fusion
  10.1 0.1 broadcast_in_dim.26
  10.2 0.6 pad_maximum_fusion
  10.8 0.0 all-gather.6.cloned.1.call-update
  10.8 39.3 %all-gather.4.cloned.1.call-done = bf16[128,4096]{1,0:T(8,128)(2,1)} async-done(((bf16[8,4096]{1,0:T(8,128)(2,1)}), bf16[128,4096]{1,0:T(8,128)(2,1)}) %all-gather.4.cloned.1.call-update) | async-done | bytes 1048592 | tf_op jit(solution)/shard_map/all_gather | solution.py:30
  50.2 1.8 %fusion.34 = f32[128,64]{0,1:T(8,128)S(1)} fusion(bf16[128,4096]{1,0:T(8,128)(2,1)} %all-gather.4.cloned.1.call-done, bf16[1,8192,64]{1,2,0:T(8,128)(2,1)} %param.10), kind=kOutput, calls=%fused_computation.24 | convolution fusion | flops 67108864 | bytes 1605632 | tf_op jit(solution)/shard_map/dot_general | solution.py:40
  52.0 37.4 %all-gather.6.cloned.1.call-done = bf16[128,4224]{1,0:T(8,128)(2,1)} async-done(((bf16[8,4224]{1,0:T(8,128)(2,1)}), bf16[128,4224]{1,0:T(8,128)(2,1)}) %all-gather.6.cloned.1.call-update) | async-done | bytes 1081360 | tf_op jit(solution)/shard_map/all_gather | solution.py:30
  89.4 0.0 copy-start.3
  89.4 1.0 fusion.38
  90.4 1.8 %fusion.29 = bf16[128,64]{0,1:T(8,128)(2,1)S(1)} fusion(f32[128,64]{0,1:T(8,128)S(1)} %fusion.34, bf16[128,4224]{1,0:T(8,128)(2,1)} %all-gather.6.cloned.1.call-done, bf16[1,8192,64]{1,2,0:T(8,128)(2,1)} %param.10, pred[128]{0:T(512)(128)(4,1)S(1)} %fusion.38), kind=kOutput, calls=%fused_computation.19 | convolution fusion | flops 67133440 | bytes 1622144 | tf_op jit(solution)/shard_map/dot_general | solution.py:40
  92.2 20.1 %all-gather = bf16[2048,64]{0,1:T(8,128)(2,1)S(1)} all-gather(bf16[128,64]{0,1:T(8,128)(2,1)S(1)} %fusion.29), channel_id=2, replica_groups=mesh['groups'=2,'tensor'=16] {'tensor'}, dimensions={0}, use_global_device_ids=true | all-gather | bytes 278528 | tf_op jit(solution)/shard_map/all_gather | solution.py:50
  112.4 6.8 %fusion = f32[128,1792]{1,0:T(8,128)S(1)} fusion(bf16[8192,1792]{1,0:T(8,128)(2,1)} %param.9, bf16[128,4224]{1,0:T(8,128)(2,1)} %all-gather.6.cloned.1.call-done), kind=kOutput, calls=%fused_computation.1 | convolution fusion | flops 1879048192 | bytes 16646144 | tf_op jit(solution)/shard_map/dot_general | solution.py:37
  119.2 0.0 copy-done.3
  119.2 0.0 copy-start.2
  119.2 6.5 %fusion.4 = f32[128,1792]{1,0:T(8,128)S(1)} fusion(bf16[8192,1792]{1,0:T(8,128)(2,1)} %param.8, bf16[128,4224]{1,0:T(8,128)(2,1)S(1)} %copy-done.3), kind=kOutput, calls=%fused_computation.5 | convolution fusion | flops 1879048192 | bytes 16646144 | tf_op jit(solution)/shard_map/dot_general | solution.py:34
  125.7 0.0 copy-done.2
  125.7 6.5 %fusion.13 = f32[128,1792]{1,0:T(8,128)S(1)} fusion(f32[128,1792]{1,0:T(8,128)S(1)} %fusion.4, bf16[128,4096]{1,0:T(8,128)(2,1)S(1)} %copy-done.2, bf16[8192,1792]{1,0:T(8,128)(2,1)} %param.8), kind=kOutput, calls=%fused_computation.12 | convolution fusion | flops 1879277568 | bytes 17563648 | tf_op jit(solution)/shard_map/dot_general | solution.py:34
  132.2 0.0 copy-start.4
  132.2 0.0 copy-start.1
  132.2 6.6 %fusion.16 = f32[128,1792]{1,0:T(8,128)S(1)} fusion(f32[128,1792]{1,0:T(8,128)S(1)} %fusion, bf16[128,4096]{1,0:T(8,128)(2,1)S(1)} %copy-done.2, bf16[8192,1792]{1,0:T(8,128)(2,1)} %param.9), kind=kOutput, calls=%fused_computation.13 | convolution fusion | flops 1879277568 | bytes 17563648 | tf_op jit(solution)/shard_map/dot_general | solution.py:37
  138.9 0.0 copy-done.4
  138.9 3.2 %fusion.25 = bf16[128,1792]{1,0:T(8,128)(2,1)} fusion(f32[128,1792]{1,0:T(8,128)S(1)} %fusion.16, bf16[16,128,64]{1,0,2:T(8,128)(2,1)S(1)} %bitcast.31, bf16[16,64,1792]{2,1,0:T(8,128)(2,1)S(1)} %copy-done.4, f32[128,1792]{1,0:T(8,128)S(1)} %fusion.13), kind=kOutput, calls=%fused_computation.16 | convolution fusion | flops 471367680 | bytes 6225920 | tf_op jit(solution)/shard_map/str,srh->th/dot_general | solution.py:51
  142.1 0.0 copy-done.1
  (2 shorter events, 0.0 us)
Async XLA Ops:
  6.5 2.3 %copy-start = (s32[16]{0:T(128)S(1)}, s32[16]{0:T(128)}, u32[]{:S(2)}) copy-start(s32[16]{0:T(128)} %param.13) | copy-start | bytes 196
  6.5 43.7 %all-gather.4.cloned.1.call-start = ((), (), s32[]{:S(2)}) async-start(), calls=%async_computation | async-start | bytes 1114112 | tf_op jit(solution)/shard_map/all_gather | solution.py:30
  8.1 81.3 %all-gather.6.cloned.1.call-start = ((), (), s32[]{:S(2)}) async-start(), calls=%async_computation.1 | async-start | bytes 1148928 | tf_op jit(solution)/shard_map/all_gather | solution.py:30
  89.4 29.8 %copy-start.3 = (bf16[128,4224]{1,0:T(8,128)(2,1)S(1)}, bf16[128,4224]{1,0:T(8,128)(2,1)}, u32[]{:S(2)}) copy-start(bf16[128,4224]{1,0:T(8,128)(2,1)} %all-gather.6.cloned.1.call-done) | copy-start | bytes 3244036
  119.2 6.6 %copy-start.2 = (bf16[128,4096]{1,0:T(8,128)(2,1)S(1)}, bf16[128,4096]{1,0:T(8,128)(2,1)}, u32[]{:S(2)}) copy-start(bf16[128,4096]{1,0:T(8,128)(2,1)} %all-gather.4.cloned.1.call-done) | copy-start | bytes 3145732
  132.2 6.7 %copy-start.4 = (bf16[16,64,1792]{2,1,0:T(8,128)(2,1)S(1)}, bf16[16,64,1792]{2,1,0:T(8,128)(2,1)}, u32[]{:S(2)}) copy-start(bf16[16,64,1792]{2,1,0:T(8,128)(2,1)} %param.11) | copy-start | bytes 11010052
  132.2 9.8 %copy-start.1 = (s32[16]{0:T(128)S(1)}, s32[16]{0:T(128)}, u32[]{:S(2)}) copy-start(s32[16]{0:T(128)} %param.13) | copy-start | bytes 196
Sparse Core Ops, SparseCore 0:
  9.5 40.6 all-gather.3
  52.4 36.9 all-gather.5
where the time goes:
time: 149 us
  waiting for transfers between devices  76.7 us (51%)
  matrix products  33.3 us (22%)
  blocking collectives  20.1 us (13%)
  between operations  13.5 us (9%)
  other arithmetic  2.93 us (2%)
  local copies, waits for them, and re-layouts  2.29 us (2%)
    all_gather x2, waiting for transfers between devices, body(): gathered = lax.all_gather(piece, 'tensor', axis=0, tiled=True)  76.7 us
    all_gather x1, blocking collectives, body(): spread = lax.all_gather(low, 'tensor', axis=0, tiled=False)  20.1 us
    dot_general x2, matrix products, body(): jnp.dot(gathered, up_weight[c * step:(c + 1) * step], preferred_element_t...  13.4 us
    dot_general x2, matrix products, body(): jnp.dot(gathered, gate_weight[c * step:(c + 1) * step], preferred_element...  13 us
    dot_general x2, matrix products, body(): jnp.dot(gathered, adapter_down_weight[0, c * step:(c + 1) * step], prefer...  3.68 us
    dot_general x1, matrix products, body(): jnp.einsum('str,srh->th', spread, adapter_up_weight, preferred_element_ty...  3.19 us
  transfers between devices with their start and end apart: 2, of which 2 were waited for; matrix products, arithmetic and copies ran while one was open for 3% of the time, Pallas kernels for 0%

commit v1 on v0

--- a/solution.py
+++ b/solution.py
@@ -5,6 +5,12 @@
 
 CHUNKS = 2
 LANES = 128
+
+
+def joined_along(blocks, dim):
+    dims = list(blocks.shape[1:])
+    dims[dim] *= blocks.shape[0]
+    return jnp.moveaxis(blocks, 0, dim).reshape(dims)
 
 
 def body(
@@ -27,7 +33,19 @@
         piece = tokens[:, c * step : (c + 1) * step]
         if c == CHUNKS - 1:
             piece = jnp.concatenate([piece, slot_cols], axis=1)
-        gathered = lax.all_gather(piece, "tensor", axis=0, tiled=True)
+        count = lax.axis_size("tensor")
+        pairs = [(i, (i + 1) % count) for i in range(count)]
+        back = [(b, a) for a, b in pairs]
+        lower, upper = ([], [])
+        for step_2 in range(count - 1):
+            if step_2 % 2 == 0:
+                lower.append(lax.ppermute(lower[-1] if lower else piece, "tensor", pairs))
+            else:
+                upper.append(lax.ppermute(upper[-1] if upper else piece, "tensor", back))
+        blocks = jnp.stack([*lower[::-1], piece, *upper])
+        shift = lax.axis_index("tensor") - len(lower)
+        blocks = blocks[(jnp.arange(count) - shift) % count]
+        gathered = joined_along(blocks, 0)
         if c == CHUNKS - 1:
             slots = gathered[:, step].astype(jnp.int32)
             gathered = gathered[:, :step]

time: 149 us -> 122 us (0.82)
  waiting for transfers between devices: 76.7 us -> 12.2 us
  starting transfers between devices: 0.04 us -> 54.2 us
  between operations: 13.5 us -> 0.35 us
  blocking collectives: 20.1 us -> 18 us
  other arithmetic: 2.93 us -> 1.39 us
    all_gather x2 -> x0, waiting for transfers between devices: 76.7 us -> none  [body(): gathered = lax.all_gather(piece, 'tensor', axis=0, tiled=True)]
    ppermute x0 -> x30, starting transfers between devices: none -> 54.2 us  [the longest x14 50.4 us: body(): upper.append(lax.ppermute(upper[-1] if upper else piece, 'tensor', back))]
    ppermute x0 -> x30, waiting for transfers between devices: none -> 12.2 us  [the longest x16 7.77 us: body(): lower.append(lax.ppermute(lower[-1] if lower else piece, 'tensor', pairs))]
    all_gather x1, blocking collectives: 20.1 us -> 18 us  [body(): spread = lax.all_gather(low, 'tensor', axis=0, tiled=False)]
    dot_general x2, matrix products: 3.68 us -> 2.09 us  [body(): jnp.dot(gathered, adapter_down_weight[0, c * step:(c + 1) * step], prefer...]
  transfers between devices with their start and end apart: 2 -> 30, of which waited for: 2 -> 8; matrix products, arithmetic and copies ran while one was open for 3% -> 2% of each run, Pallas kernels for 0% -> 0%
where the time goes in v1:
time: 122 us
  starting transfers between devices  54.2 us (44%)
  matrix products  32.3 us (26%)
  blocking collectives  18 us (15%)
  waiting for transfers between devices  12.2 us (10%)
  local copies, waits for them, and re-layouts  3.37 us (3%)
  other arithmetic  1.39 us (1%)
    ppermute x14, starting transfers between devices, body(): upper.append(lax.ppermute(upper[-1] if upper else piece, 'tensor', back))  50.4 us
    all_gather x1, blocking collectives, body(): spread = lax.all_gather(low, 'tensor', axis=0, tiled=False)  18 us
    dot_general x2, matrix products, body(): jnp.dot(gathered, up_weight[c * step:(c + 1) * step], preferred_element_t...  14.7 us
    dot_general x2, matrix products, body(): jnp.dot(gathered, gate_weight[c * step:(c + 1) * step], preferred_element...  13.1 us
    ppermute x16, waiting for transfers between devices, body(): lower.append(lax.ppermute(lower[-1] if lower else piece, 'tensor', pairs))  7.77 us
    ppermute x14, waiting for transfers between devices, body(): upper.append(lax.ppermute(upper[-1] if upper else piece, 'tensor', back))  4.47 us
    ppermute x16, starting transfers between devices, body(): lower.append(lax.ppermute(lower[-1] if lower else piece, 'tensor', pairs))  3.7 us
  transfers between devices with their start and end apart: 30, of which 8 were waited for; matrix products, arithmetic and copies ran while one was open for 2% of the time, Pallas kernels for 0%

profile of v1, /device:TPU:0, one launch (start us, length us, event | category | flops | bytes accessed | tf_op | source)
XLA Modules:
  0.0 121.8 jit_solution(17737146347545487994)
XLA Ops:
  0.0 0.9 fusion.44
  0.9 0.5 collective-permute-start
  1.4 0.7 fusion.43
  2.1 0.6 gather_fusion.1
  2.7 0.7 convert_bitcast_fusion
  3.4 0.1 broadcast_in_dim.28
  3.5 2.6 %collective-permute-start.15 = (bf16[8,4224]{1,0:T(8,128)(2,1)S(1)}, bf16[8,4224]{1,0:T(8,128)(2,1)S(1)}, u32[]{:S(2)}, u32[]{:S(2)}) collective-permute-start(bf16[8,4224]{1,0:T(8,128)(2,1)S(1)} %pad_maximum_fusion), channel_id=1, source_target_pairs={{0,1},{1,2},{2,3},{3,4},{4,5},{5,6},{6,7},{7,8},{8,9},{9,10},{10,1... | collective-permute-start | bytes 202760 | tf_op jit(solution)/shard_map/ppermute | solution.py:42
  6.1 2.2 %collective-permute-done = bf16[8,4096]{1,0:T(8,128)(2,1)S(1)} collective-permute-done((bf16[8,4096]{1,0:T(8,128)(2,1)S(1)}, bf16[8,4096]{1,0:T(8,128)(2,1)S(1)}, u32[]{:S(2)}, u32[]{:S(2)}) %collective-permute-start) | collective-permute-done | bytes 65568 | tf_op jit(solution)/shard_map/ppermute | solution.py:42
  8.4 0.0 collective-permute-start.1
  8.4 4.4 %collective-permute-start.23 = (bf16[8,4224]{1,0:T(8,128)(2,1)S(1)}, bf16[8,4224]{1,0:T(8,128)(2,1)S(1)}, u32[]{:S(2)}, u32[]{:S(2)}) collective-permute-start(bf16[8,4224]{1,0:T(8,128)(2,1)S(1)} %pad_maximum_fusion), channel_id=1, source_target_pairs={{1,0},{2,1},{3,2},{4,3},{5,4},{6,5},{7,6},{8,7},{9,8},{10,9},{11,1... | collective-permute-start | bytes 202760 | tf_op jit(solution)/shard_map/ppermute | solution.py:44
  12.8 0.0 collective-permute-start.16
  12.8 4.4 %collective-permute-start.8 = (bf16[8,4096]{1,0:T(8,128)(2,1)S(1)}, bf16[8,4096]{1,0:T(8,128)(2,1)S(1)}, u32[]{:S(2)}, u32[]{:S(2)}) collective-permute-start(bf16[8,4096]{1,0:T(8,128)(2,1)S(1)} %get-tuple-element.5), channel_id=1, source_target_pairs={{1,0},{2,1},{3,2},{4,3},{5,4},{6,5},{7,6},{8,7},{9,8},{10,9},{11,1... | collective-permute-start | bytes 196616 | tf_op jit(solution)/shard_map/ppermute | solution.py:44
  17.3 4.4 %collective-permute-start.24 = (bf16[8,4224]{1,0:T(8,128)(2,1)S(1)}, bf16[8,4224]{1,0:T(8,128)(2,1)S(1)}, u32[]{:S(2)}, u32[]{:S(2)}) collective-permute-start(bf16[8,4224]{1,0:T(8,128)(2,1)S(1)} %collective-permute-done.23), channel_id=1, source_target_pairs={{1,0},{2,1},{3,2},{4,3},{5,4},{6,5},{7,6},{8,7},{9,8},{10,9},{11,1... | collective-permute-start | bytes 202760 | tf_op jit(solution)/shard_map/ppermute | solution.py:44
  21.7 4.4 %collective-permute-start.9 = (bf16[8,4096]{1,0:T(8,128)(2,1)S(1)}, bf16[8,4096]{1,0:T(8,128)(2,1)S(1)}, u32[]{:S(2)}, u32[]{:S(2)}) collective-permute-start(bf16[8,4096]{1,0:T(8,128)(2,1)S(1)} %collective-permute-done.8), channel_id=1, source_target_pairs={{1,0},{2,1},{3,2},{4,3},{5,4},{6,5},{7,6},{8,7},{9,8},{10,9},{11,1... | collective-permute-start | bytes 196616 | tf_op jit(solution)/shard_map/ppermute | solution.py:44
  26.2 4.4 %collective-permute-start.25 = (bf16[8,4224]{1,0:T(8,128)(2,1)S(1)}, bf16[8,4224]{1,0:T(8,128)(2,1)S(1)}, u32[]{:S(2)}, u32[]{:S(2)}) collective-permute-start(bf16[8,4224]{1,0:T(8,128)(2,1)S(1)} %collective-permute-done.24), channel_id=1, source_target_pairs={{1,0},{2,1},{3,2},{4,3},{5,4},{6,5},{7,6},{8,7},{9,8},{10,9},{11,1... | collective-permute-start | bytes 202760 | tf_op jit(solution)/shard_map/ppermute | solution.py:44
  30.6 4.4 %collective-permute-start.10 = (bf16[8,4096]{1,0:T(8,128)(2,1)S(1)}, bf16[8,4096]{1,0:T(8,128)(2,1)S(1)}, u32[]{:S(2)}, u32[]{:S(2)}) collective-permute-start(bf16[8,4096]{1,0:T(8,128)(2,1)S(1)} %collective-permute-done.9), channel_id=1, source_target_pairs={{1,0},{2,1},{3,2},{4,3},{5,4},{6,5},{7,6},{8,7},{9,8},{10,9},{11,1... | collective-permute-start | bytes 196616 | tf_op jit(solution)/shard_map/ppermute | solution.py:44
  35.1 4.4 %collective-permute-start.26 = (bf16[8,4224]{1,0:T(8,128)(2,1)S(1)}, bf16[8,4224]{1,0:T(8,128)(2,1)S(1)}, u32[]{:S(2)}, u32[]{:S(2)}) collective-permute-start(bf16[8,4224]{1,0:T(8,128)(2,1)S(1)} %collective-permute-done.25), channel_id=1, source_target_pairs={{1,0},{2,1},{3,2},{4,3},{5,4},{6,5},{7,6},{8,7},{9,8},{10,9},{11,1... | collective-permute-start | bytes 202760 | tf_op jit(solution)/shard_map/ppermute | solution.py:44
  39.5 4.4 %collective-permute-start.11 = (bf16[8,4096]{1,0:T(8,128)(2,1)S(1)}, bf16[8,4096]{1,0:T(8,128)(2,1)S(1)}, u32[]{:S(2)}, u32[]{:S(2)}) collective-permute-start(bf16[8,4096]{1,0:T(8,128)(2,1)S(1)} %collective-permute-done.10), channel_id=1, source_target_pairs={{1,0},{2,1},{3,2},{4,3},{5,4},{6,5},{7,6},{8,7},{9,8},{10,9},{11,1... | collective-permute-start | bytes 196616 | tf_op jit(solution)/shard_map/ppermute | solution.py:44
  44.0 1.9 %collective-permute-done.11 = bf16[8,4096]{1,0:T(8,128)(2,1)S(1)} collective-permute-done((bf16[8,4096]{1,0:T(8,128)(2,1)S(1)}, bf16[8,4096]{1,0:T(8,128)(2,1)S(1)}, u32[]{:S(2)}, u32[]{:S(2)}) %collective-permute-start.11) | collective-permute-done | bytes 65568 | tf_op jit(solution)/shard_map/ppermute | solution.py:44
  45.9 4.5 %collective-permute-start.12 = (bf16[8,4096]{1,0:T(8,128)(2,1)S(1)}, bf16[8,4096]{1,0:T(8,128)(2,1)S(1)}, u32[]{:S(2)}, u32[]{:S(2)}) collective-permute-start(bf16[8,4096]{1,0:T(8,128)(2,1)S(1)} %collective-permute-done.11), channel_id=1, source_target_pairs={{1,0},{2,1},{3,2},{4,3},{5,4},{6,5},{7,6},{8,7},{9,8},{10,9},{11,1... | collective-permute-start | bytes 196616 | tf_op jit(solution)/shard_map/ppermute | solution.py:44
  50.4 0.0 collective-permute-start.27
  50.4 0.5 collective-permute-start.20
  50.9 0.1 collective-permute-start.6
  51.0 1.3 %collective-permute-done.12 = bf16[8,4096]{1,0:T(8,128)(2,1)S(1)} collective-permute-done((bf16[8,4096]{1,0:T(8,128)(2,1)S(1)}, bf16[8,4096]{1,0:T(8,128)(2,1)S(1)}, u32[]{:S(2)}, u32[]{:S(2)}) %collective-permute-start.12) | collective-permute-done | bytes 65568 | tf_op jit(solution)/shard_map/ppermute | solution.py:44
  52.3 4.5 %collective-permute-start.13 = (bf16[8,4096]{1,0:T(8,128)(2,1)S(1)}, bf16[8,4096]{1,0:T(8,128)(2,1)S(1)}, u32[]{:S(2)}, u32[]{:S(2)}) collective-permute-start(bf16[8,4096]{1,0:T(8,128)(2,1)S(1)} %collective-permute-done.12), channel_id=1, source_target_pairs={{1,0},{2,1},{3,2},{4,3},{5,4},{6,5},{7,6},{8,7},{9,8},{10,9},{11,1... | collective-permute-start | bytes 196616 | tf_op jit(solution)/shard_map/ppermute | solution.py:44
  56.8 0.7 collective-permute-start.28
  57.5 0.2 collective-permute-done.6
  57.7 1.0 collective-permute-done.13
  58.7 4.5 %collective-permute-start.14 = (bf16[8,4096]{1,0:T(8,128)(2,1)S(1)}, bf16[8,4096]{1,0:T(8,128)(2,1)S(1)}, u32[]{:S(2)}, u32[]{:S(2)}) collective-permute-start(bf16[8,4096]{1,0:T(8,128)(2,1)S(1)} %collective-permute-done.13), channel_id=1, source_target_pairs={{1,0},{2,1},{3,2},{4,3},{5,4},{6,5},{7,6},{8,7},{9,8},{10,9},{11,1... | collective-permute-start | bytes 196616 | tf_op jit(solution)/shard_map/ppermute | solution.py:44
  63.1 0.7 collective-permute-start.29
  63.9 0.0 collective-permute-done.21
  63.9 0.7 collective-permute-done.7
  64.8 0.2 collective-permute-done.14
  65.1 0.6 gather_fusion
  65.7 4.6 %collective-permute-done.22 = bf16[8,4224]{1,0:T(8,128)(2,1)S(1)} collective-permute-done((bf16[8,4224]{1,0:T(8,128)(2,1)S(1)}, bf16[8,4224]{1,0:T(8,128)(2,1)S(1)}, u32[]{:S(2)}, u32[]{:S(2)}) %collective-permute-start.22) | collective-permute-done | bytes 67616 | tf_op jit(solution)/shard_map/ppermute | solution.py:42
  70.6 0.7 gather_fusion.2
  71.3 0.0 copy-start.4
  71.3 0.1 copy.16
  71.4 1.6 %fusion.33 = f32[128,64]{0,1:T(8,128)S(1)} fusion(bf16[128,4224]{1,0:T(8,128)(2,1)S(1)} %bitcast.97, bf16[1,8192,64]{1,2,0:T(8,128)(2,1)} %param.10), kind=kOutput, calls=%fused_computation.25 | convolution fusion | flops 67108864 | bytes 1605632 | tf_op jit(solution)/shard_map/dot_general | solution.py:58
  73.0 0.5 fusion.29
  73.5 18.0 %all-gather = bf16[2048,64]{0,1:T(8,128)(2,1)S(1)} all-gather(bf16[128,64]{0,1:T(8,128)(2,1)S(1)} %fusion.29), channel_id=2, replica_groups=mesh['groups'=2,'tensor'=16] {'tensor'}, dimensions={0}, use_global_device_ids=true | all-gather | bytes 278528 | tf_op jit(solution)/shard_map/all_gather | solution.py:68
  91.6 6.5 %fusion = f32[128,1792]{1,0:T(8,128)S(1)} fusion(bf16[8192,1792]{1,0:T(8,128)(2,1)} %param.9, bf16[128,4224]{1,0:T(8,128)(2,1)S(1)} %bitcast.98), kind=kOutput, calls=%fused_computation.3 | convolution fusion | flops 1879048192 | bytes 16646144 | tf_op jit(solution)/shard_map/dot_general | solution.py:55
  98.0 6.5 %fusion.4 = f32[128,1792]{1,0:T(8,128)S(1)} fusion(bf16[8192,1792]{1,0:T(8,128)(2,1)} %param.8, bf16[128,4224]{1,0:T(8,128)(2,1)S(1)} %bitcast.99), kind=kOutput, calls=%fused_computation.7 | convolution fusion | flops 1879048192 | bytes 16646144 | tf_op jit(solution)/shard_map/dot_general | solution.py:52
  104.5 0.0 copy-start.2
  104.5 6.7 %fusion.13 = f32[128,1792]{1,0:T(8,128)S(1)} fusion(f32[128,1792]{1,0:T(8,128)S(1)} %fusion.4, bf16[8192,1792]{1,0:T(8,128)(2,1)} %param.8, bf16[16,8,4096]{2,1,0:T(8,128)(2,1)S(1)} %gather_fusion), kind=kOutput, calls=%fused_computation.14 | convolution fusion | flops 1879277568 | bytes 17563648 | tf_op jit(solution)/shard_map/dot_general | solution.py:52
  111.2 2.3 %fusion.10 = f32[128,1792]{1,0:T(8,128)S(1)} fusion(bf16[16,128,64]{1,0,2:T(8,128)(2,1)S(1)} %bitcast.100, bf16[16,64,1792]{2,1,0:T(8,128)(2,1)S(1)} %copy-done.2), kind=kOutput, calls=%fused_computation.13 | convolution fusion | flops 469762048 | bytes 4849664 | tf_op jit(solution)/shard_map/str,srh->th/dot_general | solution.py:69
  113.6 0.0 copy-start.1
  113.6 8.2 %fusion.25 = bf16[128,1792]{1,0:T(8,128)(2,1)} fusion(f32[128,1792]{1,0:T(8,128)S(1)} %fusion.10, f32[128,1792]{1,0:T(8,128)S(1)} %fusion, bf16[8192,1792]{1,0:T(8,128)(2,1)} %param.9, bf16[16,8,4096]{2,1,0:T(8,128)(2,1)S(1)} %gather_fusion, f32[128,1792]{1,0:T(8,128)S(1)} %fusion.13), kind=kOutput, calls=%fused_computation.18 | convolution fusion | flops 1880883200 | bytes 18939904 | tf_op jit(solution)/shard_map/dot_general | solution.py:55
  (76 shorter events, 0.5 us)
Async XLA Ops:
  0.0 2.1 %copy-start = (s32[16]{0:T(128)S(1)}, s32[16]{0:T(128)}, u32[]{:S(2)}) copy-start(s32[16]{0:T(128)} %param.13) | copy-start | bytes 196
  0.0 64.7 %copy-start.3 = (bf16[8,8192]{1,0:T(8,128)(2,1)S(1)}, bf16[8,8192]{1,0:T(8,128)(2,1)}, u32[]{:S(2)}) copy-start(bf16[8,8192]{1,0:T(8,128)(2,1)} %param.7) | copy-start | bytes 393220
  0.9 7.4 %collective-permute-start = (bf16[8,4096]{1,0:T(8,128)(2,1)S(1)}, bf16[8,4096]{1,0:T(8,128)(2,1)S(1)}, u32[]{:S(2)}, u32[]{:S(2)}) collective-permute-start(bf16[8,4096]{1,0:T(8,128)(2,1)S(1)} %get-tuple-element.5), channel_id=1, source_target_pairs={{0,1},{1,2},{2,3},{3,4},{4,5},{5,6},{6,7},{7,8},{8,9},{9,10},{10,1... | collective-permute-start | bytes 196616 | tf_op jit(solution)/shard_map/ppermute | solution.py:42
  3.5 9.3 %collective-permute-start.15 = (bf16[8,4224]{1,0:T(8,128)(2,1)S(1)}, bf16[8,4224]{1,0:T(8,128)(2,1)S(1)}, u32[]{:S(2)}, u32[]{:S(2)}) collective-permute-start(bf16[8,4224]{1,0:T(8,128)(2,1)S(1)} %pad_maximum_fusion), channel_id=1, source_target_pairs={{0,1},{1,2},{2,3},{3,4},{4,5},{5,6},{6,7},{7,8},{8,9},{9,10},{10,1... | collective-permute-start | bytes 202760 | tf_op jit(solution)/shard_map/ppermute | solution.py:42
  8.4 8.9 %collective-permute-start.1 = (bf16[8,4096]{1,0:T(8,128)(2,1)S(1)}, bf16[8,4096]{1,0:T(8,128)(2,1)S(1)}, u32[]{:S(2)}, u32[]{:S(2)}) collective-permute-start(bf16[8,4096]{1,0:T(8,128)(2,1)S(1)} %collective-permute-done), channel_id=1, source_target_pairs={{0,1},{1,2},{2,3},{3,4},{4,5},{5,6},{6,7},{7,8},{8,9},{9,10},{10,1... | collective-permute-start | bytes 196616 | tf_op jit(solution)/shard_map/ppermute | solution.py:42
  8.4 8.9 %collective-permute-start.23 = (bf16[8,4224]{1,0:T(8,128)(2,1)S(1)}, bf16[8,4224]{1,0:T(8,128)(2,1)S(1)}, u32[]{:S(2)}, u32[]{:S(2)}) collective-permute-start(bf16[8,4224]{1,0:T(8,128)(2,1)S(1)} %pad_maximum_fusion), channel_id=1, source_target_pairs={{1,0},{2,1},{3,2},{4,3},{5,4},{6,5},{7,6},{8,7},{9,8},{10,9},{11,1... | collective-permute-start | bytes 202760 | tf_op jit(solution)/shard_map/ppermute | solution.py:44
  12.8 8.9 %collective-permute-start.16 = (bf16[8,4224]{1,0:T(8,128)(2,1)S(1)}, bf16[8,4224]{1,0:T(8,128)(2,1)S(1)}, u32[]{:S(2)}, u32[]{:S(2)}) collective-permute-start(bf16[8,4224]{1,0:T(8,128)(2,1)S(1)} %collective-permute-done.15), channel_id=1, source_target_pairs={{0,1},{1,2},{2,3},{3,4},{4,5},{5,6},{6,7},{7,8},{8,9},{9,10},{10,1... | collective-permute-start | bytes 202760 | tf_op jit(solution)/shard_map/ppermute | solution.py:42
  12.8 8.9 %collective-permute-start.8 = (bf16[8,4096]{1,0:T(8,128)(2,1)S(1)}, bf16[8,4096]{1,0:T(8,128)(2,1)S(1)}, u32[]{:S(2)}, u32[]{:S(2)}) collective-permute-start(bf16[8,4096]{1,0:T(8,128)(2,1)S(1)} %get-tuple-element.5), channel_id=1, source_target_pairs={{1,0},{2,1},{3,2},{4,3},{5,4},{6,5},{7,6},{8,7},{9,8},{10,9},{11,1... | collective-permute-start | bytes 196616 | tf_op jit(solution)/shard_map/ppermute | solution.py:44
  17.3 8.9 %collective-permute-start.2 = (bf16[8,4096]{1,0:T(8,128)(2,1)S(1)}, bf16[8,4096]{1,0:T(8,128)(2,1)S(1)}, u32[]{:S(2)}, u32[]{:S(2)}) collective-permute-start(bf16[8,4096]{1,0:T(8,128)(2,1)S(1)} %collective-permute-done.1), channel_id=1, source_target_pairs={{0,1},{1,2},{2,3},{3,4},{4,5},{5,6},{6,7},{7,8},{8,9},{9,10},{10,1... | collective-permute-start | bytes 196616 | tf_op jit(solution)/shard_map/ppermute | solution.py:42
  17.3 8.9 %collective-permute-start.24 = (bf16[8,4224]{1,0:T(8,128)(2,1)S(1)}, bf16[8,4224]{1,0:T(8,128)(2,1)S(1)}, u32[]{:S(2)}, u32[]{:S(2)}) collective-permute-start(bf16[8,4224]{1,0:T(8,128)(2,1)S(1)} %collective-permute-done.23), channel_id=1, source_target_pairs={{1,0},{2,1},{3,2},{4,3},{5,4},{6,5},{7,6},{8,7},{9,8},{10,9},{11,1... | collective-permute-start | bytes 202760 | tf_op jit(solution)/shard_map/ppermute | solution.py:44
  21.7 8.9 %collective-permute-start.17 = (bf16[8,4224]{1,0:T(8,128)(2,1)S(1)}, bf16[8,4224]{1,0:T(8,128)(2,1)S(1)}, u32[]{:S(2)}, u32[]{:S(2)}) collective-permute-start(bf16[8,4224]{1,0:T(8,128)(2,1)S(1)} %collective-permute-done.16), channel_id=1, source_target_pairs={{0,1},{1,2},{2,3},{3,4},{4,5},{5,6},{6,7},{7,8},{8,9},{9,10},{10,1... | collective-permute-start | bytes 202760 | tf_op jit(solution)/shard_map/ppermute | solution.py:42
  21.7 8.9 %collective-permute-start.9 = (bf16[8,4096]{1,0:T(8,128)(2,1)S(1)}, bf16[8,4096]{1,0:T(8,128)(2,1)S(1)}, u32[]{:S(2)}, u32[]{:S(2)}) collective-permute-start(bf16[8,4096]{1,0:T(8,128)(2,1)S(1)} %collective-permute-done.8), channel_id=1, source_target_pairs={{1,0},{2,1},{3,2},{4,3},{5,4},{6,5},{7,6},{8,7},{9,8},{10,9},{11,1... | collective-permute-start | bytes 196616 | tf_op jit(solution)/shard_map/ppermute | solution.py:44
  26.2 8.9 %collective-permute-start.3 = (bf16[8,4096]{1,0:T(8,128)(2,1)S(1)}, bf16[8,4096]{1,0:T(8,128)(2,1)S(1)}, u32[]{:S(2)}, u32[]{:S(2)}) collective-permute-start(bf16[8,4096]{1,0:T(8,128)(2,1)S(1)} %collective-permute-done.2), channel_id=1, source_target_pairs={{0,1},{1,2},{2,3},{3,4},{4,5},{5,6},{6,7},{7,8},{8,9},{9,10},{10,1... | collective-permute-start | bytes 196616 | tf_op jit(solution)/shard_map/ppermute | solution.py:42
  26.2 8.9 %collective-permute-start.25 = (bf16[8,4224]{1,0:T(8,128)(2,1)S(1)}, bf16[8,4224]{1,0:T(8,128)(2,1)S(1)}, u32[]{:S(2)}, u32[]{:S(2)}) collective-permute-start(bf16[8,4224]{1,0:T(8,128)(2,1)S(1)} %collective-permute-done.24), channel_id=1, source_target_pairs={{1,0},{2,1},{3,2},{4,3},{5,4},{6,5},{7,6},{8,7},{9,8},{10,9},{11,1... | collective-permute-start | bytes 202760 | tf_op jit(solution)/shard_map/ppermute | solution.py:44
  30.6 8.9 %collective-permute-start.18 = (bf16[8,4224]{1,0:T(8,128)(2,1)S(1)}, bf16[8,4224]{1,0:T(8,128)(2,1)S(1)}, u32[]{:S(2)}, u32[]{:S(2)}) collective-permute-start(bf16[8,4224]{1,0:T(8,128)(2,1)S(1)} %collective-permute-done.17), channel_id=1, source_target_pairs={{0,1},{1,2},{2,3},{3,4},{4,5},{5,6},{6,7},{7,8},{8,9},{9,10},{10,1... | collective-permute-start | bytes 202760 | tf_op jit(solution)/shard_map/ppermute | solution.py:42
  30.6 8.9 %collective-permute-start.10 = (bf16[8,4096]{1,0:T(8,128)(2,1)S(1)}, bf16[8,4096]{1,0:T(8,128)(2,1)S(1)}, u32[]{:S(2)}, u32[]{:S(2)}) collective-permute-start(bf16[8,4096]{1,0:T(8,128)(2,1)S(1)} %collective-permute-done.9), channel_id=1, source_target_pairs={{1,0},{2,1},{3,2},{4,3},{5,4},{6,5},{7,6},{8,7},{9,8},{10,9},{11,1... | collective-permute-start | bytes 196616 | tf_op jit(solution)/shard_map/ppermute | solution.py:44
  35.1 8.9 %collective-permute-start.4 = (bf16[8,4096]{1,0:T(8,128)(2,1)S(1)}, bf16[8,4096]{1,0:T(8,128)(2,1)S(1)}, u32[]{:S(2)}, u32[]{:S(2)}) collective-permute-start(bf16[8,4096]{1,0:T(8,128)(2,1)S(1)} %collective-permute-done.3), channel_id=1, source_target_pairs={{0,1},{1,2},{2,3},{3,4},{4,5},{5,6},{6,7},{7,8},{8,9},{9,10},{10,1... | collective-permute-start | bytes 196616 | tf_op jit(solution)/shard_map/ppermute | solution.py:42
  35.1 15.3 %collective-permute-start.26 = (bf16[8,4224]{1,0:T(8,128)(2,1)S(1)}, bf16[8,4224]{1,0:T(8,128)(2,1)S(1)}, u32[]{:S(2)}, u32[]{:S(2)}) collective-permute-start(bf16[8,4224]{1,0:T(8,128)(2,1)S(1)} %collective-permute-done.25), channel_id=1, source_target_pairs={{1,0},{2,1},{3,2},{4,3},{5,4},{6,5},{7,6},{8,7},{9,8},{10,9},{11,1... | collective-permute-start | bytes 202760 | tf_op jit(solution)/shard_map/ppermute | solution.py:44
  39.5 10.9 %collective-permute-start.19 = (bf16[8,4224]{1,0:T(8,128)(2,1)S(1)}, bf16[8,4224]{1,0:T(8,128)(2,1)S(1)}, u32[]{:S(2)}, u32[]{:S(2)}) collective-permute-start(bf16[8,4224]{1,0:T(8,128)(2,1)S(1)} %collective-permute-done.18), channel_id=1, source_target_pairs={{0,1},{1,2},{2,3},{3,4},{4,5},{5,6},{6,7},{7,8},{8,9},{9,10},{10,1... | collective-permute-start | bytes 202760 | tf_op jit(solution)/shard_map/ppermute | solution.py:42
  39.5 6.3 %collective-permute-start.11 = (bf16[8,4096]{1,0:T(8,128)(2,1)S(1)}, bf16[8,4096]{1,0:T(8,128)(2,1)S(1)}, u32[]{:S(2)}, u32[]{:S(2)}) collective-permute-start(bf16[8,4096]{1,0:T(8,128)(2,1)S(1)} %collective-permute-done.10), channel_id=1, source_target_pairs={{1,0},{2,1},{3,2},{4,3},{5,4},{6,5},{7,6},{8,7},{9,8},{10,9},{11,1... | collective-permute-start | bytes 196616 | tf_op jit(solution)/shard_map/ppermute | solution.py:44
  44.0 6.9 %collective-permute-start.5 = (bf16[8,4096]{1,0:T(8,128)(2,1)S(1)}, bf16[8,4096]{1,0:T(8,128)(2,1)S(1)}, u32[]{:S(2)}, u32[]{:S(2)}) collective-permute-start(bf16[8,4096]{1,0:T(8,128)(2,1)S(1)} %collective-permute-done.4), channel_id=1, source_target_pairs={{0,1},{1,2},{2,3},{3,4},{4,5},{5,6},{6,7},{7,8},{8,9},{9,10},{10,1... | collective-permute-start | bytes 196616 | tf_op jit(solution)/shard_map/ppermute | solution.py:42
  45.9 6.4 %collective-permute-start.12 = (bf16[8,4096]{1,0:T(8,128)(2,1)S(1)}, bf16[8,4096]{1,0:T(8,128)(2,1)S(1)}, u32[]{:S(2)}, u32[]{:S(2)}) collective-permute-start(bf16[8,4096]{1,0:T(8,128)(2,1)S(1)} %collective-permute-done.11), channel_id=1, source_target_pairs={{1,0},{2,1},{3,2},{4,3},{5,4},{6,5},{7,6},{8,7},{9,8},{10,9},{11,1... | collective-permute-start | bytes 196616 | tf_op jit(solution)/shard_map/ppermute | solution.py:44
  50.4 6.4 %collective-permute-start.27 = (bf16[8,4224]{1,0:T(8,128)(2,1)S(1)}, bf16[8,4224]{1,0:T(8,128)(2,1)S(1)}, u32[]{:S(2)}, u32[]{:S(2)}) collective-permute-start(bf16[8,4224]{1,0:T(8,128)(2,1)S(1)} %collective-permute-done.26), channel_id=1, source_target_pairs={{1,0},{2,1},{3,2},{4,3},{5,4},{6,5},{7,6},{8,7},{9,8},{10,9},{11,1... | collective-permute-start | bytes 202760 | tf_op jit(solution)/shard_map/ppermute | solution.py:44
  50.4 7.1 %collective-permute-start.20 = (bf16[8,4224]{1,0:T(8,128)(2,1)S(1)}, bf16[8,4224]{1,0:T(8,128)(2,1)S(1)}, u32[]{:S(2)}, u32[]{:S(2)}) collective-permute-start(bf16[8,4224]{1,0:T(8,128)(2,1)S(1)} %collective-permute-done.19), channel_id=1, source_target_pairs={{0,1},{1,2},{2,3},{3,4},{4,5},{5,6},{6,7},{7,8},{8,9},{9,10},{10,1... | collective-permute-start | bytes 202760 | tf_op jit(solution)/shard_map/ppermute | solution.py:42
  50.9 6.8 %collective-permute-start.6 = (bf16[8,4096]{1,0:T(8,128)(2,1)S(1)}, bf16[8,4096]{1,0:T(8,128)(2,1)S(1)}, u32[]{:S(2)}, u32[]{:S(2)}) collective-permute-start(bf16[8,4096]{1,0:T(8,128)(2,1)S(1)} %collective-permute-done.5), channel_id=1, source_target_pairs={{0,1},{1,2},{2,3},{3,4},{4,5},{5,6},{6,7},{7,8},{8,9},{9,10},{10,1... | collective-permute-start | bytes 196616 | tf_op jit(solution)/shard_map/ppermute | solution.py:42
  52.3 6.4 %collective-permute-start.13 = (bf16[8,4096]{1,0:T(8,128)(2,1)S(1)}, bf16[8,4096]{1,0:T(8,128)(2,1)S(1)}, u32[]{:S(2)}, u32[]{:S(2)}) collective-permute-start(bf16[8,4096]{1,0:T(8,128)(2,1)S(1)} %collective-permute-done.12), channel_id=1, source_target_pairs={{1,0},{2,1},{3,2},{4,3},{5,4},{6,5},{7,6},{8,7},{9,8},{10,9},{11,1... | collective-permute-start | bytes 196616 | tf_op jit(solution)/shard_map/ppermute | solution.py:44
  56.8 6.4 %collective-permute-start.28 = (bf16[8,4224]{1,0:T(8,128)(2,1)S(1)}, bf16[8,4224]{1,0:T(8,128)(2,1)S(1)}, u32[]{:S(2)}, u32[]{:S(2)}) collective-permute-start(bf16[8,4224]{1,0:T(8,128)(2,1)S(1)} %collective-permute-done.27), channel_id=1, source_target_pairs={{1,0},{2,1},{3,2},{4,3},{5,4},{6,5},{7,6},{8,7},{9,8},{10,9},{11,1... | collective-permute-start | bytes 202760 | tf_op jit(solution)/shard_map/ppermute | solution.py:44
  57.5 6.4 %collective-permute-start.21 = (bf16[8,4224]{1,0:T(8,128)(2,1)S(1)}, bf16[8,4224]{1,0:T(8,128)(2,1)S(1)}, u32[]{:S(2)}, u32[]{:S(2)}) collective-permute-start(bf16[8,4224]{1,0:T(8,128)(2,1)S(1)} %collective-permute-done.20), channel_id=1, source_target_pairs={{0,1},{1,2},{2,3},{3,4},{4,5},{5,6},{6,7},{7,8},{8,9},{9,10},{10,1... | collective-permute-start | bytes 202760 | tf_op jit(solution)/shard_map/ppermute | solution.py:42
  57.6 6.9 %collective-permute-start.7 = (bf16[8,4096]{1,0:T(8,128)(2,1)S(1)}, bf16[8,4096]{1,0:T(8,128)(2,1)S(1)}, u32[]{:S(2)}, u32[]{:S(2)}) collective-permute-start(bf16[8,4096]{1,0:T(8,128)(2,1)S(1)} %collective-permute-done.6), channel_id=1, source_target_pairs={{0,1},{1,2},{2,3},{3,4},{4,5},{5,6},{6,7},{7,8},{8,9},{9,10},{10,1... | collective-permute-start | bytes 196616 | tf_op jit(solution)/shard_map/ppermute | solution.py:42
  58.7 6.4 %collective-permute-start.14 = (bf16[8,4096]{1,0:T(8,128)(2,1)S(1)}, bf16[8,4096]{1,0:T(8,128)(2,1)S(1)}, u32[]{:S(2)}, u32[]{:S(2)}) collective-permute-start(bf16[8,4096]{1,0:T(8,128)(2,1)S(1)} %collective-permute-done.13), channel_id=1, source_target_pairs={{1,0},{2,1},{3,2},{4,3},{5,4},{6,5},{7,6},{8,7},{9,8},{10,9},{11,1... | collective-permute-start | bytes 196616 | tf_op jit(solution)/shard_map/ppermute | solution.py:44
  63.1 7.4 %collective-permute-start.29 = (bf16[8,4224]{1,0:T(8,128)(2,1)S(1)}, bf16[8,4224]{1,0:T(8,128)(2,1)S(1)}, u32[]{:S(2)}, u32[]{:S(2)}) collective-permute-start(bf16[8,4224]{1,0:T(8,128)(2,1)S(1)} %collective-permute-done.28), channel_id=1, source_target_pairs={{1,0},{2,1},{3,2},{4,3},{5,4},{6,5},{7,6},{8,7},{9,8},{10,9},{11,1... | collective-permute-start | bytes 202760 | tf_op jit(solution)/shard_map/ppermute | solution.py:44
  63.9 6.4 %collective-permute-start.22 = (bf16[8,4224]{1,0:T(8,128)(2,1)S(1)}, bf16[8,4224]{1,0:T(8,128)(2,1)S(1)}, u32[]{:S(2)}, u32[]{:S(2)}) collective-permute-start(bf16[8,4224]{1,0:T(8,128)(2,1)S(1)} %collective-permute-done.21), channel_id=1, source_target_pairs={{0,1},{1,2},{2,3},{3,4},{4,5},{5,6},{6,7},{7,8},{8,9},{9,10},{10,1... | collective-permute-start | bytes 202760 | tf_op jit(solution)/shard_map/ppermute | solution.py:42
  71.3 1.7 %copy-start.4 = (bf16[1,8192,64]{1,2,0:T(8,128)(2,1)S(1)}, bf16[1,8192,64]{1,2,0:T(8,128)(2,1)}, u32[]{:S(2)}) copy-start(bf16[1,8192,64]{1,2,0:T(8,128)(2,1)} %param.10) | copy-start | bytes 3145732
  104.5 6.7 %copy-start.2 = (bf16[16,64,1792]{2,1,0:T(8,128)(2,1)S(1)}, bf16[16,64,1792]{2,1,0:T(8,128)(2,1)}, u32[]{:S(2)}) copy-start(bf16[16,64,1792]{2,1,0:T(8,128)(2,1)} %param.11) | copy-start | bytes 11010052
  113.6 8.3 %copy-start.1 = (s32[16]{0:T(128)S(1)}, s32[16]{0:T(128)}, u32[]{:S(2)}) copy-start(s32[16]{0:T(128)} %param.13) | copy-start | bytes 196
